TPU v7x, 32 devices: a whole 2x2x4 slice. The times are simulated.
32 devices in a mesh: row: 4 (over x, core), col: 8 (over z, y).
Axes of the slice: x: 2, y: 2, z: 4, core: 2. Of those that a mesh axis runs over, the one named last changes fastest.
Arguments:
- right_side: float32 [64, 16384], P(None, 'row'), may hold values from -8 to 8
- blocks: bfloat16 [3072, 128, 128], P(('row', 'col')), may hold values from -1 to 1
- targets: int32 [3072, 1], P(('row', 'col')), may hold values from 0 to 7; in each aligned block of 96 rows (0 to 95, 96 to 191, ...) at most 24 rows name the same one
- tile_rows: int32 [3072], P(('row', 'col')), may hold values from 0 to 31
- tile_cols: int32 [3072], P(('row', 'col')), may hold values from 0 to 31
Outputs:
- solution: float32 [64, 8, 4096], P(None, 'col', 'row')
- phibar: float32 [64], replicated
Inputs may be any that keep to these rules, and one draw needn't show every extreme that they name: `targets`: among the 96 blocks of one device, at most 24 name the same grid column, and some grid column is named exactly 24 times by some device.
All inputs are finite; a program needn't handle non-finite values.
Results may differ from a plain program's by a relative error of at most 0.0032.
Values may be sent and summed in bfloat16 or wider, within the bound.
No kernel may reach another device: no remote copies, remote signals or barrier semaphores. Data moves between devices by JAX's collectives and lax.ppermute only.
A program may use at most 128 MiB of HBM per device.

v0:
```python
import jax
import jax.numpy as jnp
from jax import lax
from jax.sharding import PartitionSpec as P

TC = 32
ITERS = 4
EPSILON = 1e-06


def gather_tiles(vector_bf, indices, block_size):
    snapshots, extent = vector_bf.shape
    vector_tiles = vector_bf.reshape(snapshots, extent // block_size, block_size)
    return jnp.take(vector_tiles, indices, axis=1)


def place_terms(weighted, indices, n_out):
    snapshots, number, block_size = weighted.shape
    onehot = (indices[:, None] == jnp.arange(n_out, dtype=jnp.int32)[None, :]).astype(jnp.float32)
    summed = jnp.einsum("ksi,st->kti", weighted, onehot, precision=lax.Precision.HIGHEST)
    return summed.reshape(snapshots, n_out * block_size)


def forward_terms(vector_bf, blocks, row_index, col_index, n_out):
    picked = gather_tiles(vector_bf, col_index, blocks.shape[1])
    weighted = jnp.einsum("sij,ksj->ksi", blocks, picked, preferred_element_type=jnp.float32)
    return place_terms(weighted, row_index, n_out)


def backward_terms(vector_bf, blocks, row_index, col_index, n_out):
    picked = gather_tiles(vector_bf, row_index, blocks.shape[1])
    weighted = jnp.einsum("sji,ksj->ksi", blocks, picked, preferred_element_type=jnp.float32)
    return place_terms(weighted, col_index, n_out)


def per_device(right_side, blocks, targets, tile_rows, tile_cols):
    col_count = lax.axis_size("col")
    row_count = lax.axis_size("row")
    block_size = blocks.shape[1]
    snapshots = right_side.shape[0]
    row_tiles = right_side.shape[1] // block_size
    own_count = blocks.shape[0]
    capacity = 2 * own_count // col_count
    target = targets[:, 0]
    matches = (target[:, None] == jnp.arange(col_count, dtype=jnp.int32)[None, :]).astype(jnp.int32)
    before = jnp.cumsum(matches, axis=0) - matches
    slot_index = target * capacity + jnp.sum(before * matches, axis=1)
    outgoing = (
        jnp.zeros((col_count * capacity, block_size, block_size), blocks.dtype)
        .at[slot_index]
        .set(blocks)
    )
    places = (
        jnp.zeros((col_count * capacity, 2), jnp.int32)
        .at[slot_index]
        .set(jnp.stack([tile_rows, tile_cols], axis=1))
    )
    arrived, arrived_places = (
        lax.all_to_all(
            outgoing.reshape(col_count, capacity, block_size, block_size),
            "col",
            split_axis=0,
            concat_axis=0,
            tiled=True,
        ),
        lax.all_to_all(
            places.reshape(col_count, capacity, 2), "col", split_axis=0, concat_axis=0, tiled=True
        ),
    )
    work_blocks = arrived.reshape(col_count * capacity, block_size, block_size)
    flat_places = arrived_places.reshape(col_count * capacity, 2)
    work_rows = flat_places[:, 0]
    work_cols = flat_places[:, 1]

    def backward(left_bf):
        return backward_terms(left_bf, work_blocks, work_rows, work_cols, TC)

    def sum_right(partial_value):
        return lax.psum(partial_value, "row")

    def finish_left(unscaled, need_form):
        squares = jnp.sum(unscaled * unscaled, axis=1)
        total = lax.psum(squares, "row")
        beta_norm = jnp.sqrt(total + EPSILON)
        scaled = unscaled / beta_norm[:, None]
        rounded = None
        if need_form:
            rounded = scaled.astype(jnp.bfloat16)
        return (beta_norm, scaled, rounded)

    def finish_right(unscaled):
        squares = jnp.sum(unscaled * unscaled, axis=1)
        total = lax.psum(squares, "col")
        alpha_norm = jnp.sqrt(total + EPSILON)
        scaled = unscaled / alpha_norm[:, None]
        rounded = scaled.astype(jnp.bfloat16)
        return (alpha_norm, scaled, rounded)

    beta_norm, left_vec, left_bf = finish_left(right_side, True)
    alpha_norm, right_vec, right_bf = finish_right(sum_right(backward(left_bf)))
    search = right_vec
    solution = jnp.zeros_like(right_vec)
    phibar = beta_norm
    rhobar = alpha_norm
    for iteration in range(ITERS):
        last_turn = iteration + 1 == ITERS
        unscaled = (
            lax.psum(forward_terms(right_bf, work_blocks, work_rows, work_cols, row_tiles), "col")
            - alpha_norm[:, None] * left_vec
        )
        beta_norm, left_vec, left_bf = finish_left(unscaled, not last_turn)
        rho_value = jnp.sqrt(rhobar * rhobar + beta_norm * beta_norm)
        cosine = rhobar / rho_value
        sine_value = beta_norm / rho_value
        phi_value = cosine * phibar
        phibar = sine_value * phibar
        solution = solution + (phi_value / rho_value)[:, None] * search
        if not last_turn:
            unscaled = sum_right(backward(left_bf)) - beta_norm[:, None] * right_vec
            alpha_norm, right_vec, right_bf = finish_right(unscaled)
            theta_value = sine_value * alpha_norm
            rhobar = -cosine * alpha_norm
            search = right_vec - (theta_value / rho_value)[:, None] * search
    share_len = solution.shape[1] // row_count
    solution = lax.dynamic_slice_in_dim(solution, lax.axis_index("row") * share_len, share_len, 1)
    return (solution.reshape(snapshots, 1, solution.shape[1]), phibar)


def solution(mesh):
    placed = (
        P(None, "row"),
        P(("row", "col"), None, None),
        P(("row", "col"), None),
        P(("row", "col")),
        P(("row", "col")),
    )
    return jax.shard_map(
        per_device,
        mesh=mesh,
        in_specs=placed,
        out_specs=(P(None, "col", "row"), P()),
        check_vma=False,
    )
```

profile of v0, /device:TPU:0, one launch (start us, length us, event | category | flops | bytes accessed | tf_op | source)
XLA Modules:
  0.0 906.9 jit_solution(17280355181446882380)
XLA Ops:
  11.9 7.3 all-to-all-start
  23.4 14.7 %scatter_fusion = bf16[192,128,128]{2,1,0:T(8,128)(2,1)} fusion(bf16[192,128,128]{2,1,0:T(8,128)(2,1)} %broadcast_in_dim.14, s32[96]{0:T(128)S(1)} %fusion.105, bf16[96,128,128]{2,1,0:T(8,128)(2,1)} %param.8), kind=kCustom, calls=%fused_computation.9 | custom fusion | bytes 9437568 | tf_op jit(solution)/shard_map/scatter | solution.py:51
  38.1 6.1 all-to-all-start.1
  44.4 5.7 psum.119
  53.3 128.6 %all-to-all-done.1 = bf16[8,24,128,128]{3,2,1,0:T(8,128)(2,1)} async-done(((bf16[8,24,128,128]{3,2,1,0:T(8,128)(2,1)}), bf16[8,24,128,128]{3,2,1,0:T(8,128)(2,1)}, u32[]{:S(2)}, u32[]{:S(2)}) %all-to-all-start.1) | async-done | bytes 6291488 | tf_op jit(solution)/shard_map/all_to_all | solution.py:59
  187.5 5.7 fusion.14
  194.9 35.2 %all-reduce.9.cloned.1.call-done = f32[64,4096]{1,0:T(8,128)} async-done(((f32[64,4096]{1,0:T(8,128)}), f32[64,4096]{1,0:T(8,128)}) %all-reduce.9.cloned.1.call-update) | async-done | bytes 1048592 | tf_op jit(solution)/shard_map/psum | solution.py:79
  231.5 21.5 %psum.121 = f32[64]{0:T(128)S(1)} all-reduce(f32[64]{0:T(128)S(1)} %multiply_reduce_fusion.7), channel_id=1, replica_groups=mesh['row'=4,'col'=8] {'col'}, use_global_device_ids=true, to_apply=%region_8.10 | all-reduce | flops 64 | bytes 512 | tf_op jit(solution)/shard_map/psum | solution.py:93
  257.4 8.1 fusion.51
  265.4 5.7 fusion.12
  272.8 75.0 %all-reduce.11.cloned.1.call-done = f32[64,4096]{1,0:T(8,128)} async-done(((f32[64,4096]{1,0:T(8,128)}), f32[64,4096]{1,0:T(8,128)}) %all-reduce.11.cloned.1.call-update) | async-done | bytes 1048592 | tf_op jit(solution)/shard_map/psum | solution.py:108
  350.4 6.1 psum.123
  373.7 35.8 %all-reduce.13.cloned.1.call-done = f32[64,4096]{1,0:T(8,128)} async-done(((f32[64,4096]{1,0:T(8,128)}), f32[64,4096]{1,0:T(8,128)}) %all-reduce.13.cloned.1.call-update) | async-done | bytes 1048592 | tf_op jit(solution)/shard_map/psum | solution.py:79
  411.0 21.8 %psum.125 = f32[64]{0:T(128)S(1)} all-reduce(f32[64]{0:T(128)S(1)} %multiply_reduce_fusion.5), channel_id=1, replica_groups=mesh['row'=4,'col'=8] {'col'}, use_global_device_ids=true, to_apply=%region_14.16 | all-reduce | flops 64 | bytes 512 | tf_op jit(solution)/shard_map/psum | solution.py:93
  437.2 8.1 fusion.57
  445.3 5.8 fusion.8
  452.8 75.0 %all-reduce.15.cloned.1.call-done = f32[64,4096]{1,0:T(8,128)} async-done(((f32[64,4096]{1,0:T(8,128)}), f32[64,4096]{1,0:T(8,128)}) %all-reduce.15.cloned.1.call-update) | async-done | bytes 1048592 | tf_op jit(solution)/shard_map/psum | solution.py:108
  530.3 6.1 psum.127
  546.1 5.8 fusion.6
  553.6 35.8 %all-reduce.17.cloned.1.call-done = f32[64,4096]{1,0:T(8,128)} async-done(((f32[64,4096]{1,0:T(8,128)}), f32[64,4096]{1,0:T(8,128)}) %all-reduce.17.cloned.1.call-update) | async-done | bytes 1048592 | tf_op jit(solution)/shard_map/psum | solution.py:79
  591.0 21.6 %psum.129 = f32[64]{0:T(128)S(1)} all-reduce(f32[64]{0:T(128)S(1)} %multiply_reduce_fusion.3), channel_id=1, replica_groups=mesh['row'=4,'col'=8] {'col'}, use_global_device_ids=true, to_apply=%region_20.22 | all-reduce | flops 64 | bytes 512 | tf_op jit(solution)/shard_map/psum | solution.py:93
  617.9 8.1 fusion.63
  626.0 5.8 fusion.4
  633.5 75.0 %all-reduce.19.cloned.1.call-done = f32[64,4096]{1,0:T(8,128)} async-done(((f32[64,4096]{1,0:T(8,128)}), f32[64,4096]{1,0:T(8,128)}) %all-reduce.19.cloned.1.call-update) | async-done | bytes 1048592 | tf_op jit(solution)/shard_map/psum | solution.py:108
  711.0 6.3 psum.131
  727.1 5.8 fusion.2
  734.5 35.8 %all-reduce.21.cloned.1.call-done = f32[64,4096]{1,0:T(8,128)} async-done(((f32[64,4096]{1,0:T(8,128)}), f32[64,4096]{1,0:T(8,128)}) %all-reduce.21.cloned.1.call-update) | async-done | bytes 1048592 | tf_op jit(solution)/shard_map/psum | solution.py:79
  771.9 21.5 %psum.133 = f32[64]{0:T(128)S(1)} all-reduce(f32[64]{0:T(128)S(1)} %multiply_reduce_fusion.1), channel_id=1, replica_groups=mesh['row'=4,'col'=8] {'col'}, use_global_device_ids=true, to_apply=%region_26.28 | all-reduce | flops 64 | bytes 512 | tf_op jit(solution)/shard_map/psum | solution.py:93
  798.8 8.1 fusion.69
  806.9 5.8 fusion
  814.4 75.1 %all-reduce.23.cloned.1.call-done = f32[64,4096]{1,0:T(8,128)} async-done(((f32[64,4096]{1,0:T(8,128)}), f32[64,4096]{1,0:T(8,128)}) %all-reduce.23.cloned.1.call-update) | async-done | bytes 1048592 | tf_op jit(solution)/shard_map/psum | solution.py:108
  891.0 5.9 psum.135
  (100 shorter events, 103.6 us)
Async XLA Ops:
  11.9 26.2 %all-to-all-start = ((s32[8,24,2]{1,2,0:T(2,128)}), s32[8,24,2]{1,2,0:T(2,128)S(1)}, u32[]{:S(2)}, u32[]{:S(2)}) async-start(s32[8,24,2]{1,2,0:T(2,128)} %copy.46), calls=%async_computation | async-start | bytes 16384 | tf_op jit(solution)/shard_map/all_to_all | solution.py:66
  38.1 6.1 copy-start.1
  38.1 143.8 %all-to-all-start.1 = ((bf16[8,24,128,128]{3,2,1,0:T(8,128)(2,1)}), bf16[8,24,128,128]{3,2,1,0:T(8,128)(2,1)}, u32[]{:S(2)}, u32[]{:S(2)}) async-start(bf16[8,24,128,128]{3,2,1,0:T(8,128)(2,1)} %bitcast.172), calls=%async_computation.1 | async-start | bytes 12582912 | tf_op jit(solution)/shard_map/all_to_all | solution.py:59
  44.2 185.9 %all-reduce.9.cloned.1.call-start = ((), (), s32[]{:S(2)}) async-start(), calls=%async_computation.2 | async-start | bytes 2097152 | tf_op jit(solution)/shard_map/psum | solution.py:79
  194.8 153.0 %all-reduce.11.cloned.1.call-start = ((), (), s32[]{:S(2)}) async-start(), calls=%async_computation.3 | async-start | bytes 2097152 | tf_op jit(solution)/shard_map/psum | solution.py:108
  272.8 136.7 %all-reduce.13.cloned.1.call-start = ((), (), s32[]{:S(2)}) async-start(), calls=%async_computation.4 | async-start | bytes 2097152 | tf_op jit(solution)/shard_map/psum | solution.py:79
  373.6 154.1 %all-reduce.15.cloned.1.call-start = ((), (), s32[]{:S(2)}) async-start(), calls=%async_computation.5 | async-start | bytes 2097152 | tf_op jit(solution)/shard_map/psum | solution.py:108
  451.1 76.6 %copy-start.4 = (f32[64,4096]{1,0:T(8,128)S(1)}, f32[64,4096]{1,0:T(8,128)}, u32[]{:S(2)}) copy-start(f32[64,4096]{1,0:T(8,128)} %get-tuple-element.25) | copy-start | bytes 3145732
  452.7 136.7 %all-reduce.17.cloned.1.call-start = ((), (), s32[]{:S(2)}) async-start(), calls=%async_computation.6 | async-start | bytes 2097152 | tf_op jit(solution)/shard_map/psum | solution.py:79
  553.5 154.9 %all-reduce.19.cloned.1.call-start = ((), (), s32[]{:S(2)}) async-start(), calls=%async_computation.7 | async-start | bytes 2097152 | tf_op jit(solution)/shard_map/psum | solution.py:108
  631.8 76.6 %copy-start.3 = (f32[64,4096]{1,0:T(8,128)S(1)}, f32[64,4096]{1,0:T(8,128)}, u32[]{:S(2)}) copy-start(f32[64,4096]{1,0:T(8,128)} %get-tuple-element.21) | copy-start | bytes 3145732
  633.4 136.9 %all-reduce.21.cloned.1.call-start = ((), (), s32[]{:S(2)}) async-start(), calls=%async_computation.8 | async-start | bytes 2097152 | tf_op jit(solution)/shard_map/psum | solution.py:79
  732.9 37.5 %copy-start = (f32[64,4096]{1,0:T(8,128)S(1)}, f32[64,4096]{1,0:T(8,128)}, u32[]{:S(2)}) copy-start(f32[64,4096]{1,0:T(8,128)} %get-tuple-element.19) | copy-start | bytes 3145732
  734.5 155.0 %all-reduce.23.cloned.1.call-start = ((), (), s32[]{:S(2)}) async-start(), calls=%async_computation.9 | async-start | bytes 2097152 | tf_op jit(solution)/shard_map/psum | solution.py:108
  812.7 76.8 %copy-start.2 = (f32[64,4096]{1,0:T(8,128)S(1)}, f32[64,4096]{1,0:T(8,128)}, u32[]{:S(2)}) copy-start(f32[64,4096]{1,0:T(8,128)} %get-tuple-element.17) | copy-start | bytes 3145732
Sparse Core Ops, SparseCore 0:
  194.9 35.0 all-reduce.8
  272.9 74.8 all-reduce.10
  373.7 35.7 all-reduce.12
  452.9 74.8 all-reduce.14
  553.7 35.7 all-reduce.16
  633.5 74.8 all-reduce.18
  734.6 35.7 all-reduce.20
  814.5 74.9 all-reduce.22
where the time goes:
time: 916 us; the launch traced here: 907 us
  waiting for transfers between devices  571 us (62%)
  blocking collectives  116 us (13%)
  matrix products  101 us (11%)
  local copies, waits for them, and re-layouts  56.9 us (6%)
  other arithmetic  32.9 us (4%)
  between operations  14.7 us (2%)
  starting transfers between devices  13.7 us (1%)
    psum x4, waiting for transfers between devices, per_device(): lax.psum(forward_terms(right_bf, work_blocks, work_rows, work_cols, row_t...  300 us
    psum x4, waiting for transfers between devices, sum_right(): return lax.psum(partial_value, 'row')  143 us
    all_to_all x1, waiting for transfers between devices, per_device(): lax.all_to_all(outgoing.reshape(col_count, capacity, block_size, block_si...  129 us
    psum x4, blocking collectives, finish_right(): total = lax.psum(squares, 'col')  86.4 us
    dot_general x8, matrix products, place_terms(): jnp.einsum('ksi,st->kti', weighted, onehot, precision=lax.Precision.HIGHEST)  46.2 us
    dot_general x4, matrix products, forward_terms(): jnp.einsum('sij,ksj->ksi', blocks, picked, preferred_element_type=jnp.flo...  32.3 us
    psum x5, blocking collectives, finish_left(): total = lax.psum(squares, 'row')  30.1 us
    dot_general x4, matrix products, backward_terms(): jnp.einsum('sji,ksj->ksi', blocks, picked, preferred_element_type=jnp.flo...  22.3 us
  transfers between devices with their start and end apart: 10, of which 9 were waited for; matrix products, arithmetic and copies ran while one was open for 2% of the time, Pallas kernels for 0%

commit v1 on v0

--- a/solution.py
+++ b/solution.py
@@ -2,10 +2,15 @@
 import jax.numpy as jnp
 from jax import lax
 from jax.sharding import PartitionSpec as P
+from jax.lax import all_gather
 
 TC = 32
 ITERS = 4
 EPSILON = 1e-06
+
+
+def _advance_zones(state):
+    return jnp.sum(all_gather(state, "col"), axis=0)
 
 
 def gather_tiles(vector_bf, indices, block_size):
@@ -105,7 +110,7 @@
     for iteration in range(ITERS):
         last_turn = iteration + 1 == ITERS
         unscaled = (
-            lax.psum(forward_terms(right_bf, work_blocks, work_rows, work_cols, row_tiles), "col")
+            _advance_zones(forward_terms(right_bf, work_blocks, work_rows, work_cols, row_tiles))
             - alpha_norm[:, None] * left_vec
         )
         beta_norm, left_vec, left_bf = finish_left(unscaled, not last_turn)

time: 916 us -> 1120 us (1.22)
  waiting for transfers between devices: 571 us -> 754 us
  other arithmetic: 32.9 us -> 52.9 us
    all_gather x0 -> x4, waiting for transfers between devices: none -> 487 us  [_advance_zones(): return jnp.sum(all_gather(state, 'col'), axis=0)]
    psum x4 -> x0, waiting for transfers between devices: 300 us -> none  [per_device(): lax.psum(forward_terms(right_bf, work_blocks, work_rows, work_cols, row_t...]
    reduce_sum x0 -> x4, other arithmetic: none -> 19.9 us  [_advance_zones(): return jnp.sum(all_gather(state, 'col'), axis=0)]
where the time goes in v1:
time: 1120 us; the launch traced here: 1110 us
  waiting for transfers between devices  754 us (67%)
  blocking collectives  118 us (11%)
  matrix products  102 us (9%)
  local copies, waits for them, and re-layouts  56.4 us (5%)
  other arithmetic  52.9 us (5%)
  between operations  14.7 us (1%)
  starting transfers between devices  13.8 us (1%)
    all_gather x4, waiting for transfers between devices, _advance_zones(): return jnp.sum(all_gather(state, 'col'), axis=0)  487 us
    psum x4, waiting for transfers between devices, sum_right(): return lax.psum(partial_value, 'row')  138 us
    all_to_all x1, waiting for transfers between devices, per_device(): lax.all_to_all(outgoing.reshape(col_count, capacity, block_size, block_si...  129 us
    psum x4, blocking collectives, finish_right(): total = lax.psum(squares, 'col')  86.4 us
    dot_general x8, matrix products, place_terms(): jnp.einsum('ksi,st->kti', weighted, onehot, precision=lax.Precision.HIGHEST)  47 us
    dot_general x4, matrix products, forward_terms(): jnp.einsum('sij,ksj->ksi', blocks, picked, preferred_element_type=jnp.flo...  32.3 us
    psum x5, blocking collectives, finish_left(): total = lax.psum(squares, 'row')  31.1 us
  transfers between devices with their start and end apart: 10, of which 9 were waited for; matrix products, arithmetic and copies ran while one was open for 2% of the time, Pallas kernels for 0%

profile of v1, /device:TPU:0, one launch (start us, length us, event | category | flops | bytes accessed | tf_op | source)
XLA Modules:
  0.0 1110.3 jit_solution(16508610900727394507)
XLA Ops:
  11.9 7.3 all-to-all-start
  23.4 14.7 %scatter_fusion = bf16[192,128,128]{2,1,0:T(8,128)(2,1)} fusion(bf16[192,128,128]{2,1,0:T(8,128)(2,1)} %broadcast_in_dim.14, s32[96]{0:T(128)S(1)} %fusion.117, bf16[96,128,128]{2,1,0:T(8,128)(2,1)} %param.8), kind=kCustom, calls=%fused_computation.9 | custom fusion | bytes 9437568 | tf_op jit(solution)/shard_map/scatter | solution.py:56
  38.1 6.1 all-to-all-start.1
  53.2 128.7 %all-to-all-done.1 = bf16[8,24,128,128]{3,2,1,0:T(8,128)(2,1)} async-done(((bf16[8,24,128,128]{3,2,1,0:T(8,128)(2,1)}), bf16[8,24,128,128]{3,2,1,0:T(8,128)(2,1)}, u32[]{:S(2)}, u32[]{:S(2)}) %all-to-all-start.1) | async-done | bytes 6291488 | tf_op jit(solution)/shard_map/all_to_all | solution.py:64
  187.4 5.7 fusion.14
  194.9 35.2 %all-reduce.5.cloned.1.call-done = f32[64,4096]{1,0:T(8,128)} async-done(((f32[64,4096]{1,0:T(8,128)}), f32[64,4096]{1,0:T(8,128)}) %all-reduce.5.cloned.1.call-update) | async-done | bytes 1048592 | tf_op jit(solution)/shard_map/psum | solution.py:84
  231.5 21.5 %psum.93 = f32[64]{0:T(128)S(1)} all-reduce(f32[64]{0:T(128)S(1)} %multiply_reduce_fusion.7), channel_id=1, replica_groups=mesh['row'=4,'col'=8] {'col'}, use_global_device_ids=true, to_apply=%region_8.10 | all-reduce | flops 64 | bytes 512 | tf_op jit(solution)/shard_map/psum | solution.py:98
  257.4 8.1 fusion.51
  265.5 6.7 fusion.80
  274.7 121.8 %all-gather.5.cloned.1.call-done = f32[8,64,4096]{2,1,0:T(8,128)} async-done(((f32[1,64,4096]{2,1,0:T(8,128)}), f32[8,64,4096]{2,1,0:T(8,128)}) %all-gather.5.cloned.1.call-update) | async-done | bytes 8388624 | tf_op jit(solution)/shard_map/all_gather | solution.py:13
  404.0 6.4 psum.94
  420.1 5.8 fusion.10
  427.6 34.1 %all-reduce.7.cloned.1.call-done = f32[64,4096]{1,0:T(8,128)} async-done(((f32[64,4096]{1,0:T(8,128)}), f32[64,4096]{1,0:T(8,128)}) %all-reduce.7.cloned.1.call-update) | async-done | bytes 1048592 | tf_op jit(solution)/shard_map/psum | solution.py:84
  463.2 21.8 %psum.96 = f32[64]{0:T(128)S(1)} all-reduce(f32[64]{0:T(128)S(1)} %multiply_reduce_fusion.5), channel_id=1, replica_groups=mesh['row'=4,'col'=8] {'col'}, use_global_device_ids=true, to_apply=%region_14.16 | all-reduce | flops 64 | bytes 512 | tf_op jit(solution)/shard_map/psum | solution.py:98
  489.4 8.1 fusion.57
  497.5 5.7 fusion.83
  504.5 121.8 %all-gather.7.cloned.1.call-done = f32[8,64,4096]{2,1,0:T(8,128)} async-done(((f32[1,64,4096]{2,1,0:T(8,128)}), f32[8,64,4096]{2,1,0:T(8,128)}) %all-gather.7.cloned.1.call-update) | async-done | bytes 8388624 | tf_op jit(solution)/shard_map/all_gather | solution.py:13
  633.8 6.3 psum.97
  649.9 5.8 fusion.6
  657.3 34.1 %all-reduce.9.cloned.1.call-done = f32[64,4096]{1,0:T(8,128)} async-done(((f32[64,4096]{1,0:T(8,128)}), f32[64,4096]{1,0:T(8,128)}) %all-reduce.9.cloned.1.call-update) | async-done | bytes 1048592 | tf_op jit(solution)/shard_map/psum | solution.py:84
  693.0 21.6 %psum.99 = f32[64]{0:T(128)S(1)} all-reduce(f32[64]{0:T(128)S(1)} %multiply_reduce_fusion.3), channel_id=1, replica_groups=mesh['row'=4,'col'=8] {'col'}, use_global_device_ids=true, to_apply=%region_20.22 | all-reduce | flops 64 | bytes 512 | tf_op jit(solution)/shard_map/psum | solution.py:98
  719.9 8.1 fusion.63
  728.0 5.7 fusion.86
  735.0 121.8 %all-gather.9.cloned.1.call-done = f32[8,64,4096]{2,1,0:T(8,128)} async-done(((f32[1,64,4096]{2,1,0:T(8,128)}), f32[8,64,4096]{2,1,0:T(8,128)}) %all-gather.9.cloned.1.call-update) | async-done | bytes 8388624 | tf_op jit(solution)/shard_map/all_gather | solution.py:13
  864.3 6.6 psum.100
  880.6 5.8 fusion.2
  888.1 34.1 %all-reduce.11.cloned.1.call-done = f32[64,4096]{1,0:T(8,128)} async-done(((f32[64,4096]{1,0:T(8,128)}), f32[64,4096]{1,0:T(8,128)}) %all-reduce.11.cloned.1.call-update) | async-done | bytes 1048592 | tf_op jit(solution)/shard_map/psum | solution.py:84
  923.7 21.5 %psum.102 = f32[64]{0:T(128)S(1)} all-reduce(f32[64]{0:T(128)S(1)} %multiply_reduce_fusion.1), channel_id=1, replica_groups=mesh['row'=4,'col'=8] {'col'}, use_global_device_ids=true, to_apply=%region_26.28 | all-reduce | flops 64 | bytes 512 | tf_op jit(solution)/shard_map/psum | solution.py:98
  950.6 8.1 fusion.69
  958.7 5.7 fusion.89
  965.7 121.8 %all-gather.11.cloned.1.call-done = f32[8,64,4096]{2,1,0:T(8,128)} async-done(((f32[1,64,4096]{2,1,0:T(8,128)}), f32[8,64,4096]{2,1,0:T(8,128)}) %all-gather.11.cloned.1.call-update) | async-done | bytes 8388624 | tf_op jit(solution)/shard_map/all_gather | solution.py:13
  1094.2 6.2 psum.103
  (104 shorter events, 123.1 us)
Async XLA Ops:
  11.9 26.2 %all-to-all-start = ((s32[8,24,2]{1,2,0:T(2,128)}), s32[8,24,2]{1,2,0:T(2,128)S(1)}, u32[]{:S(2)}, u32[]{:S(2)}) async-start(s32[8,24,2]{1,2,0:T(2,128)} %copy.46), calls=%async_computation | async-start | bytes 16384 | tf_op jit(solution)/shard_map/all_to_all | solution.py:71
  38.1 6.2 copy-start.1
  38.1 143.8 %all-to-all-start.1 = ((bf16[8,24,128,128]{3,2,1,0:T(8,128)(2,1)}), bf16[8,24,128,128]{3,2,1,0:T(8,128)(2,1)}, u32[]{:S(2)}, u32[]{:S(2)}) async-start(bf16[8,24,128,128]{3,2,1,0:T(8,128)(2,1)} %bitcast.160), calls=%async_computation.1 | async-start | bytes 12582912 | tf_op jit(solution)/shard_map/all_to_all | solution.py:64
  44.2 185.9 %all-reduce.5.cloned.1.call-start = ((), (), s32[]{:S(2)}) async-start(), calls=%async_computation.2 | async-start | bytes 2097152 | tf_op jit(solution)/shard_map/psum | solution.py:84
  194.8 201.7 %all-gather.5.cloned.1.call-start = ((), (), s32[]{:S(2)}) async-start(), calls=%async_computation.3 | async-start | bytes 9437184 | tf_op jit(solution)/shard_map/all_gather | solution.py:13
  274.7 187.1 %all-reduce.7.cloned.1.call-start = ((), (), s32[]{:S(2)}) async-start(), calls=%async_computation.4 | async-start | bytes 2097152 | tf_op jit(solution)/shard_map/psum | solution.py:84
  427.6 198.7 %all-gather.7.cloned.1.call-start = ((), (), s32[]{:S(2)}) async-start(), calls=%async_computation.5 | async-start | bytes 9437184 | tf_op jit(solution)/shard_map/all_gather | solution.py:13
  504.4 126.8 %copy-start.4 = (f32[64,4096]{1,0:T(8,128)S(1)}, f32[64,4096]{1,0:T(8,128)}, u32[]{:S(2)}) copy-start(f32[64,4096]{1,0:T(8,128)} %get-tuple-element.25) | copy-start | bytes 3145732
  504.4 187.0 %all-reduce.9.cloned.1.call-start = ((), (), s32[]{:S(2)}) async-start(), calls=%async_computation.6 | async-start | bytes 2097152 | tf_op jit(solution)/shard_map/psum | solution.py:84
  657.3 199.5 %all-gather.9.cloned.1.call-start = ((), (), s32[]{:S(2)}) async-start(), calls=%async_computation.7 | async-start | bytes 9437184 | tf_op jit(solution)/shard_map/all_gather | solution.py:13
  734.9 126.8 %copy-start.3 = (f32[64,4096]{1,0:T(8,128)S(1)}, f32[64,4096]{1,0:T(8,128)}, u32[]{:S(2)}) copy-start(f32[64,4096]{1,0:T(8,128)} %get-tuple-element.21) | copy-start | bytes 3145732
  734.9 187.3 %all-reduce.11.cloned.1.call-start = ((), (), s32[]{:S(2)}) async-start(), calls=%async_computation.8 | async-start | bytes 2097152 | tf_op jit(solution)/shard_map/psum | solution.py:84
  886.4 35.8 %copy-start = (f32[64,4096]{1,0:T(8,128)S(1)}, f32[64,4096]{1,0:T(8,128)}, u32[]{:S(2)}) copy-start(f32[64,4096]{1,0:T(8,128)} %get-tuple-element.19) | copy-start | bytes 3145732
  888.0 199.6 %all-gather.11.cloned.1.call-start = ((), (), s32[]{:S(2)}) async-start(), calls=%async_computation.9 | async-start | bytes 9437184 | tf_op jit(solution)/shard_map/all_gather | solution.py:13
  965.7 126.9 %copy-start.2 = (f32[64,4096]{1,0:T(8,128)S(1)}, f32[64,4096]{1,0:T(8,128)}, u32[]{:S(2)}) copy-start(f32[64,4096]{1,0:T(8,128)} %get-tuple-element.17) | copy-start | bytes 3145732
Sparse Core Ops, SparseCore 0:
  195.0 35.1 all-reduce.4
  274.8 121.6 all-gather.4
  427.7 33.9 all-reduce.6
  504.5 121.6 all-gather.6
  657.4 33.9 all-reduce.8
  735.0 121.6 all-gather.8
  888.1 34.0 all-reduce.10
  965.8 121.6 all-gather.10
